TPU v7x, 32 devices: a whole 2x2x4 slice. The times are simulated.
32 devices in a mesh: rec: 2 (over y), gx: 16 (over z, x, core).
Axes of the slice: x: 2, y: 2, z: 4, core: 2. Of those that a mesh axis runs over, the one named last changes fastest.
Arguments:
- velocity: float32 [4, 3, 96, 16, 128], P(None, None, ('rec', 'gx')), parts along dimension 2, may hold values from -6 to 36, as said below
- span_rim: float32 [4, 2, 96, 10, 6], P(None, None, ('rec', 'gx')), parts along dimension 2, may hold values from -6 to 36, as said below
- sketch_old: bfloat16 [3, 96, 10, 128, 256], P(None, ('rec', 'gx')), parts along dimension 1, as said below
- omega: float32 [4, 256], replicated, may hold values from -6 to 6
Outputs:
- basis: bfloat16 [3, 96, 10, 128, 256], P(None, ('rec', 'gx')), parts along dimension 1
- factor: float32 [512, 256], P('rec'), parts along dimension 0
There are 2 independent parts, one for each index of `rec`. A program takes and returns all parts, laid end to end along the dimension named above; an argument that names none is the same for every part. Nothing has to cross between parts.
Inputs may be any that keep to these rules, and one draw needn't show every extreme that they name: `sketch_old`: finite values of order one; rows differ in scale. `velocity`: finite values. `span_rim`: finite values.
All inputs are finite; a program needn't handle non-finite values.
Results may differ from a plain program's by a relative error of at most 0.014.
The roundings to bfloat16 on the way count: a program that leaves them out, or rounds other values in their place, can miss the bound.
Values sent between devices are 32-bit elements; how exact they have to be, the bound alone decides.
No kernel may reach another device: no remote copies, remote signals or barrier semaphores. Data moves between devices by JAX's collectives and lax.ppermute only.
A program may use at most 64 MiB of HBM per device.

v0:
```python
import jax
import jax.numpy as jnp
from jax import lax
from jax.sharding import PartitionSpec as P

COEFS = (0.75, -0.15, 1.0 / 60.0)


def extended_2(cells, sides, width):
    for axis, dim in sides:
        count = lax.axis_size(axis)
        head = lax.slice_in_dim(cells, 0, width, axis=dim)
        tail = lax.slice_in_dim(cells, cells.shape[dim] - width, cells.shape[dim], axis=dim)
        cells = jnp.concatenate(
            [
                lax.ppermute(tail, axis, [(i, (i + 1) % count) for i in range(count)]),
                cells,
                lax.ppermute(head, axis, [((i + 1) % count, i) for i in range(count)]),
            ],
            axis=dim,
        )
    return cells


def band_diff(padded, axis, count):
    out_shape = list(padded.shape)
    out_shape[axis] = count
    total = jnp.zeros(tuple(out_shape), jnp.float32)
    for shift_k, weight in zip((1, 2, 3), COEFS):
        ahead = lax.slice_in_dim(padded, 3 + shift_k, 3 + shift_k + count, axis=axis)
        behind = lax.slice_in_dim(padded, 3 - shift_k, 3 - shift_k + count, axis=axis)
        total = total + weight * (ahead - behind)
    return total


def span_extend(field, rim_part):
    return jnp.concatenate([rim_part[..., :3], field, rim_part[..., 3:]], axis=-1)


def upper_factor(gram):
    order = gram.shape[0]
    index = jnp.arange(order, dtype=jnp.int32)

    def column_step(j, lower):
        pick = (index == j).astype(gram.dtype)
        row = jnp.dot(pick, lower, precision=lax.Precision.HIGHEST)
        column = jnp.dot(gram, pick, precision=lax.Precision.HIGHEST) - jnp.dot(
            lower, row, precision=lax.Precision.HIGHEST
        )
        pivot = jnp.sqrt(jnp.sum(column * pick))
        below = (index > j).astype(gram.dtype)
        fresh = column * below / pivot + pick * pivot
        return lower + fresh[:, None] * pick[None, :]

    lower = lax.fori_loop(0, order, column_step, jnp.zeros_like(gram))
    return lower.T


def inverse_upper(upper):
    order = upper.shape[0]
    index = jnp.arange(order, dtype=jnp.int32)
    lower = upper.T

    def row_step(j, solved):
        pick = (index == j).astype(upper.dtype)
        row = jnp.dot(pick, lower, precision=lax.Precision.HIGHEST)
        pivot = jnp.sum(row * pick)
        fresh = (pick - jnp.dot(row, solved, precision=lax.Precision.HIGHEST)) / pivot
        return solved + pick[:, None] * fresh[None, :]

    solved = lax.fori_loop(0, order, row_step, jnp.zeros_like(upper))
    return solved.T


def gram_of(matrix):
    return lax.dot_general(
        matrix, matrix, (((0,), (0,)), ((), ())), preferred_element_type=jnp.float32
    )


def local(velocity, span_rim, sketch_old, omega):
    slabs = velocity.shape[2]
    band_rows = velocity.shape[3] - 6
    span_cells = velocity.shape[4]
    extended = extended_2(velocity, (("gx", 2),), 3)
    v_ext = extended[:, 1, :, 3 : 3 + band_rows]
    w_ext = extended[:, 2, :, 3 : 3 + band_rows]
    band = velocity[:, :, :, 3 : 3 + band_rows]
    u_span = span_extend(band[:, 0], span_rim[:, 0])
    v_span = span_extend(band[:, 1], span_rim[:, 1])
    vort_x = band_diff(velocity[:, 2], 2, band_rows) - band_diff(v_span, 3, span_cells)
    vort_y = band_diff(u_span, 3, span_cells) - band_diff(w_ext, 1, slabs)
    vort_z = band_diff(v_ext, 1, slabs) - band_diff(velocity[:, 0], 2, band_rows)
    vort = jnp.stack([vort_x, vort_y, vort_z], axis=1)
    sketch = sketch_old.astype(jnp.float32)
    for snap in range(vort.shape[0]):
        sketch = sketch + vort[snap][..., None] * omega[snap]
    sketch = sketch.astype(jnp.bfloat16)
    matrix = sketch.reshape(-1, sketch.shape[-1])
    total = jnp.float32(matrix.shape[0] * lax.axis_size("gx"))
    local_gram = gram_of(matrix) / total
    gram = lax.psum(local_gram, "gx")
    lower = lax.linalg.cholesky(gram, symmetrize_input=False)
    factor = lower.T
    eye = jnp.eye(gram.shape[0], dtype=gram.dtype)
    lower_inv = lax.linalg.triangular_solve(lower, eye, left_side=True, lower=True)
    inverse_one = lower_inv.T.astype(jnp.bfloat16)
    basis = jnp.dot(matrix, inverse_one, preferred_element_type=jnp.float32).astype(jnp.bfloat16)
    return (basis.reshape(sketch.shape), factor)


def solution(mesh):
    in_specs = (
        P(None, None, ("rec", "gx"), None, None),
        P(None, None, ("rec", "gx"), None, None),
        P(None, ("rec", "gx"), None, None, None),
        P(),
    )
    out_specs = (P(None, ("rec", "gx"), None, None, None), P("rec", None))
    return jax.shard_map(local, mesh=mesh, in_specs=in_specs, out_specs=out_specs, check_vma=False)
```

profile of v0, /device:TPU:1, one launch (start us, length us, event | category | flops | bytes accessed | tf_op | source)
XLA Modules:
  0.0 201.3 jit_solution(16693057301777906816)
XLA Ops:
  7.2 0.0 all-reduce.3.cloned.1.call-start
  7.2 0.1 collective-permute-start.1
  7.3 2.6 %collective-permute-start = (f32[4,3,3,16,128]{4,3,2,1,0:T(8,128)}, f32[4,3,3,16,128]{4,3,2,1,0:T(8,128)S(1)}, u32[]{:S(2)}, u32[]{:S(2)}) collective-permute-start(f32[4,3,3,16,128]{4,3,2,1,0:T(8,128)} %param.4), channel_id=1, source_target_pairs={{0,1},{1,2},{2,3},{3,4},{4,5},{5,6},{6,7},{7,8},{8,9},{9,10},{10,1... | collective-permute-start | bytes 884744 | tf_op jit(solution)/shard_map/ppermute | solution.py:16
  9.9 1.0 slice_bitcast_fusion.5
  10.9 1.0 slice_bitcast_fusion.4
  11.9 1.0 fusion.64
  13.0 0.2 copy.20
  13.1 0.2 copy.21
  13.3 0.4 fusion.26
  13.6 0.8 fusion.67
  14.5 0.2 copy.24
  14.7 0.2 copy.25
  14.8 0.0 copy-start.1
  14.8 2.3 %collective-permute-done = f32[4,3,3,16,128]{4,3,2,1,0:T(8,128)S(1)} collective-permute-done((f32[4,3,3,16,128]{4,3,2,1,0:T(8,128)}, f32[4,3,3,16,128]{4,3,2,1,0:T(8,128)S(1)}, u32[]{:S(2)}, u32[]{:S(2)}) %collective-permute-start) | collective-permute-done | bytes 294944 | tf_op jit(solution)/shard_map/ppermute | solution.py:16
  17.1 1.0 constant_dynamic-update-slice_fusion.1
  18.1 0.0 collective-permute-done.1
  18.2 0.1 fusion.35
  18.3 0.3 fusion.14
  18.7 0.0 copy-done.1
  18.7 7.5 %add_convert_fusion = bf16[3,3,10,128,256]{4,3,2,1,0:T(8,128)(2,1)S(1)} fusion(bf16[3,3,10,128,256]{4,3,2,1,0:T(8,128)(2,1)S(1)} %copy-done.1, f32[256]{0:T(256)S(1)} %bitcast.90, f32[3,3,10,128]{3,2,1,0:T(8,128)S(1)} %get-tuple-element.27, f32[256]{0:T(256)S(1)} %bitcast.91, f32[3,3,10,128]{3,2,1,0:T(8,128)S(1)} %get-tuple-element.28, f32[256]{0:T(256)S(1)} %bitcast.89, ...), kind=kLoop, calls=%fused_computation.3 | loop fusion | flops 29491200 | bytes 11984896 | tf_op jit(solution)/shard_map/convert_element_type | solution.py:98
  26.3 0.0 copy-start
  26.3 2.5 %copy-done = bf16[3,3,10,128,256]{4,3,2,1,0:T(8,128)(2,1)} copy-done((bf16[3,3,10,128,256]{4,3,2,1,0:T(8,128)(2,1)}, bf16[3,3,10,128,256]{4,3,2,1,0:T(8,128)(2,1)S(1)}, u32[]{:S(2)}) %copy-start) | copy-done | bytes 5898264
  28.8 2.4 %fusion = f32[256,256]{1,0:T(8,128)} fusion(bf16[3,3,10,128,256]{4,3,2,1,0:T(8,128)(2,1)S(1)} %add_convert_fusion), kind=kOutput, calls=%fused_computation.5 | convolution fusion | flops 1510014976 | bytes 6160384 | tf_op jit(solution)/shard_map/dot_general | solution.py:76
  31.2 0.0 all-reduce.3.cloned.1.call-update
  31.3 91.7 %all-reduce.3.cloned.1.call-done = f32[256,256]{1,0:T(8,128)} async-done(((f32[256,256]{1,0:T(8,128)}), f32[256,256]{1,0:T(8,128)}) %all-reduce.3.cloned.1.call-update) | async-done | bytes 262160 | tf_op jit(solution)/shard_map/psum | solution.py:102
  123.0 0.8 cholesky.118
  123.8 11.7 %cholesky.50 = f32[128,128]{1,0:T(8,128)S(1)} custom-call(f32[128,128]{1,0:T(8,128)S(1)} %cholesky.118), custom_call_target="Cholesky" | custom-call | tf_op jit(solution)/shard_map/cholesky | solution.py:103
  135.6 0.6 compare_reduce_fusion.1
  136.2 9.8 %custom-call.11 = f32[1,128,128]{1,2,0:T(8,128)S(1)} custom-call(f32[1,128,128]{2,1,0:T(8,128)S(1)} %get-tuple-element.41), custom_call_target="InvertDiagBlocksLowerTriangular" | custom-call | tf_op jit(solution)/shard_map/cholesky | solution.py:103
  146.1 1.0 constant_dynamic-update-slice_fusion.4
  147.1 1.1 convolution_subtract_fusion.1
  148.2 11.7 %cholesky.105 = f32[128,128]{1,0:T(8,128)S(1)} custom-call(f32[128,128]{1,0:T(8,128)S(1)} %convolution_subtract_fusion.1), custom_call_target="Cholesky" | custom-call | tf_op jit(solution)/shard_map/cholesky | solution.py:103
  160.0 0.7 compare_reduce_fusion
  162.0 1.0 copy.29
  163.0 0.1 triangular_solve.63
  163.0 3.8 %while.1 = (s32[]{:T(128)}, f32[256,256]{1,0:T(8,128)S(1)}, s32[2,2]{1,0:T(2,128)S(1)}, f32[2,128,128]{2,1,0:T(8,128)S(1)}, s32[]{:T(128)}) while((s32[]{:T(128)}, f32[256,256]{1,0:T(8,128)S(1)}, s32[2,2]{1,0:T(2,128)S(1)}, f32[2,128,128]{2,1,0:T(8,128)S(1)}, s32[]{:T(128)}) %tuple.43), condition=%wide.while_cond, body=%wide.while_body.sunk | while | flops 2 | bytes 131189 | solution.py:106
  163.0 0.6 fusion.77
  163.7 1.3 bitcast_dynamic-update-slice_fusion.2
  165.0 0.6 fusion.77
  165.6 1.3 bitcast_dynamic-update-slice_fusion.2
  166.9 19.7 %custom-call.12 = f32[2,128,128]{1,2,0:T(8,128)S(1)} custom-call(f32[2,128,128]{2,1,0:T(8,128)S(1)} %get-tuple-element.9), custom_call_target="InvertDiagBlocksLowerTriangular" | custom-call | tf_op jit(solution)/shard_map/triangular_solve | solution.py:106
  186.6 0.3 fusion.68
  186.8 0.3 convolution_subtract_fusion
  187.1 0.3 convolution_convert_fusion.1
  187.4 7.0 %convolution_convert_fusion = bf16[11520,256]{1,0:T(8,128)(2,1)} fusion(bf16[11520,256]{1,0:T(8,128)(2,1)} %bitcast.86, bf16[128,256]{1,0:T(8,128)(2,1)S(1)} %convolution_convert_fusion.1, bf16[128,256]{1,0:T(8,128)(2,1)S(1)} %get-tuple-element.52), kind=kOutput, calls=%fused_computation.2 | convolution fusion | flops 1513160704 | bytes 11927552 | tf_op jit(solution)/shard_map/dot_general | solution.py:108
  (17 shorter events, 0.3 us)
Async XLA Ops:
  7.2 115.8 %all-reduce.3.cloned.1.call-start = ((), (), s32[]{:S(2)}) async-start(), calls=%async_computation | async-start | bytes 524288 | tf_op jit(solution)/shard_map/psum | solution.py:102
  7.2 10.9 %collective-permute-start.1 = (f32[4,3,3,16,128]{4,3,2,1,0:T(8,128)}, f32[4,3,3,16,128]{4,3,2,1,0:T(8,128)S(1)}, u32[]{:S(2)}, u32[]{:S(2)}) collective-permute-start(f32[4,3,3,16,128]{4,3,2,1,0:T(8,128)} %param.4), channel_id=1, source_target_pairs={{1,0},{2,1},{3,2},{4,3},{5,4},{6,5},{7,6},{8,7},{9,8},{10,9},{11,1... | collective-permute-start | bytes 884744 | tf_op jit(solution)/shard_map/ppermute | solution.py:18
  7.3 9.8 %collective-permute-start = (f32[4,3,3,16,128]{4,3,2,1,0:T(8,128)}, f32[4,3,3,16,128]{4,3,2,1,0:T(8,128)S(1)}, u32[]{:S(2)}, u32[]{:S(2)}) collective-permute-start(f32[4,3,3,16,128]{4,3,2,1,0:T(8,128)} %param.4), channel_id=1, source_target_pairs={{0,1},{1,2},{2,3},{3,4},{4,5},{5,6},{6,7},{7,8},{8,9},{9,10},{10,1... | collective-permute-start | bytes 884744 | tf_op jit(solution)/shard_map/ppermute | solution.py:16
  14.8 3.9 %copy-start.1 = (bf16[3,3,10,128,256]{4,3,2,1,0:T(8,128)(2,1)S(1)}, bf16[3,3,10,128,256]{4,3,2,1,0:T(8,128)(2,1)}, u32[]{:S(2)}) copy-start(bf16[3,3,10,128,256]{4,3,2,1,0:T(8,128)(2,1)} %param.6) | copy-start | bytes 17694724
  26.3 2.5 %copy-start = (bf16[3,3,10,128,256]{4,3,2,1,0:T(8,128)(2,1)}, bf16[3,3,10,128,256]{4,3,2,1,0:T(8,128)(2,1)S(1)}, u32[]{:S(2)}) copy-start(bf16[3,3,10,128,256]{4,3,2,1,0:T(8,128)(2,1)S(1)} %add_convert_fusion) | copy-start | bytes 17694724
Sparse Core Ops, SparseCore 0:
  31.4 91.5 all-reduce.2
where the time goes:
time: 202 us; the launch traced here: 201 us
  waiting for transfers between devices  94 us (47%)
  other arithmetic  62.7 us (31%)
  between operations  15.5 us (8%)
  local copies, waits for them, and re-layouts  13.9 us (7%)
  matrix products  12.4 us (6%)
  starting transfers between devices  2.76 us (1%)
    psum x1, waiting for transfers between devices, local(): gram = lax.psum(local_gram, 'gx')  91.7 us
    another operation x7, other arithmetic, local(): lower = lax.linalg.cholesky(gram, symmetrize_input=False)  34.6 us
    another operation x2, other arithmetic, local(): lax.linalg.triangular_solve(lower, eye, left_side=True, lower=True)  19.7 us
    convert_element_type x1, other arithmetic, local(): sketch = sketch.astype(jnp.bfloat16)  7.55 us
    dot_general x1, matrix products, local(): jnp.dot(matrix, inverse_one, preferred_element_type=jnp.float32)  6.98 us
    unnamed x7, local copies, waits for them, and re-layouts  4.54 us
  transfers between devices with their start and end apart: 3, of which 2 were waited for; matrix products, arithmetic and copies ran while one was open for 3% of the time, Pallas kernels for 0%

commit v1 on v0

--- a/solution.py
+++ b/solution.py
@@ -2,8 +2,14 @@
 import jax.numpy as jnp
 from jax import lax
 from jax.sharding import PartitionSpec as P
+from jax.lax import all_gather
 
 COEFS = (0.75, -0.15, 1.0 / 60.0)
+
+
+def trace_face(patch):
+    t_next = jnp.sum(all_gather(patch, "gx"), axis=0)
+    return t_next
 
 
 def extended_2(cells, sides, width):
@@ -99,7 +105,7 @@
     matrix = sketch.reshape(-1, sketch.shape[-1])
     total = jnp.float32(matrix.shape[0] * lax.axis_size("gx"))
     local_gram = gram_of(matrix) / total
-    gram = lax.psum(local_gram, "gx")
+    gram = trace_face(local_gram)
     lower = lax.linalg.cholesky(gram, symmetrize_input=False)
     factor = lower.T
     eye = jnp.eye(gram.shape[0], dtype=gram.dtype)

time: 202 us -> 163 us (0.81)
  waiting for transfers between devices: 94 us -> 55.5 us
  other arithmetic: 62.7 us -> 65.3 us
    psum x1 -> x0, waiting for transfers between devices: 91.7 us -> none  [local(): gram = lax.psum(local_gram, 'gx')]
    all_gather x0 -> x1, waiting for transfers between devices: none -> 53.2 us  [trace_face(): t_next = jnp.sum(all_gather(patch, 'gx'), axis=0)]
    reduce_sum x0 -> x1, other arithmetic: none -> 2.48 us  [trace_face(): t_next = jnp.sum(all_gather(patch, 'gx'), axis=0)]
  transfers between devices with their start and end apart: 3 -> 3, of which waited for: 2 -> 2; matrix products, arithmetic and copies ran while one was open for 3% -> 4% of each run, Pallas kernels for 0% -> 0%
where the time goes in v1:
time: 163 us
  other arithmetic  65.3 us (40%)
  waiting for transfers between devices  55.5 us (34%)
  between operations  15.5 us (10%)
  local copies, waits for them, and re-layouts  12.9 us (8%)
  matrix products  10.7 us (7%)
  starting transfers between devices  2.76 us (2%)
    all_gather x1, waiting for transfers between devices, trace_face(): t_next = jnp.sum(all_gather(patch, 'gx'), axis=0)  53.2 us
    another operation x7, other arithmetic, local(): lower = lax.linalg.cholesky(gram, symmetrize_input=False)  34.7 us
    another operation x2, other arithmetic, local(): lax.linalg.triangular_solve(lower, eye, left_side=True, lower=True)  19.7 us
    convert_element_type x1, other arithmetic, local(): sketch = sketch.astype(jnp.bfloat16)  7.55 us
    dot_general x1, matrix products, local(): jnp.dot(matrix, inverse_one, preferred_element_type=jnp.float32)  6.98 us
    unnamed x7, local copies, waits for them, and re-layouts  4.36 us
    another operation x6, local copies, waits for them, and re-layouts  3.81 us
  transfers between devices with their start and end apart: 3, of which 2 were waited for; matrix products, arithmetic and copies ran while one was open for 4% of the time, Pallas kernels for 0%

profile of v1, /device:TPU:1, one launch (start us, length us, event | category | flops | bytes accessed | tf_op | source)
XLA Modules:
  0.0 162.7 jit_solution(17976625191389136886)
XLA Ops:
  7.2 0.0 all-gather.3.cloned.1.call-start
  7.2 0.1 collective-permute-start.1
  7.3 2.6 %collective-permute-start = (f32[4,3,3,16,128]{4,3,2,1,0:T(8,128)}, f32[4,3,3,16,128]{4,3,2,1,0:T(8,128)S(1)}, u32[]{:S(2)}, u32[]{:S(2)}) collective-permute-start(f32[4,3,3,16,128]{4,3,2,1,0:T(8,128)} %param.4), channel_id=1, source_target_pairs={{0,1},{1,2},{2,3},{3,4},{4,5},{5,6},{6,7},{7,8},{8,9},{9,10},{10,1... | collective-permute-start | bytes 884744 | tf_op jit(solution)/shard_map/ppermute | solution.py:22
  9.9 1.0 slice_bitcast_fusion.5
  10.9 1.0 slice_bitcast_fusion.4
  11.9 1.0 fusion.64
  13.0 0.2 copy.20
  13.1 0.2 copy.21
  13.3 0.4 fusion.26
  13.6 0.8 fusion.67
  14.5 0.2 copy.24
  14.7 0.2 copy.25
  14.8 0.0 copy-start.1
  14.8 2.3 %collective-permute-done = f32[4,3,3,16,128]{4,3,2,1,0:T(8,128)S(1)} collective-permute-done((f32[4,3,3,16,128]{4,3,2,1,0:T(8,128)}, f32[4,3,3,16,128]{4,3,2,1,0:T(8,128)S(1)}, u32[]{:S(2)}, u32[]{:S(2)}) %collective-permute-start) | collective-permute-done | bytes 294944 | tf_op jit(solution)/shard_map/ppermute | solution.py:22
  17.1 1.0 constant_dynamic-update-slice_fusion.1
  18.1 0.0 collective-permute-done.1
  18.2 0.1 fusion.35
  18.3 0.3 fusion.14
  18.7 0.0 copy-done.1
  18.7 7.5 %add_convert_fusion = bf16[3,3,10,128,256]{4,3,2,1,0:T(8,128)(2,1)S(1)} fusion(bf16[3,3,10,128,256]{4,3,2,1,0:T(8,128)(2,1)S(1)} %copy-done.1, f32[256]{0:T(256)S(1)} %bitcast.92, f32[3,3,10,128]{3,2,1,0:T(8,128)S(1)} %get-tuple-element.27, f32[256]{0:T(256)S(1)} %bitcast.93, f32[3,3,10,128]{3,2,1,0:T(8,128)S(1)} %get-tuple-element.28, f32[256]{0:T(256)S(1)} %bitcast.91, ...), kind=kLoop, calls=%fused_computation.3 | loop fusion | flops 29491200 | bytes 11984896 | tf_op jit(solution)/shard_map/convert_element_type | solution.py:104
  26.3 0.0 copy-start
  26.3 2.5 %copy-done = bf16[3,3,10,128,256]{4,3,2,1,0:T(8,128)(2,1)} copy-done((bf16[3,3,10,128,256]{4,3,2,1,0:T(8,128)(2,1)}, bf16[3,3,10,128,256]{4,3,2,1,0:T(8,128)(2,1)S(1)}, u32[]{:S(2)}) %copy-start) | copy-done | bytes 5898264
  28.8 2.4 %fusion = f32[256,256]{1,0:T(8,128)} fusion(bf16[3,3,10,128,256]{4,3,2,1,0:T(8,128)(2,1)S(1)} %add_convert_fusion), kind=kOutput, calls=%fused_computation.5 | convolution fusion | flops 1510014976 | bytes 6160384 | tf_op jit(solution)/shard_map/dot_general | solution.py:82
  31.2 0.0 all-gather.3.cloned.1.call-update
  31.3 53.2 %all-gather.3.cloned.1.call-done = f32[4096,256]{1,0:T(8,128)} async-done(((f32[256,256]{1,0:T(8,128)}), f32[4096,256]{1,0:T(8,128)}) %all-gather.3.cloned.1.call-update) | async-done | bytes 4194320 | tf_op jit(solution)/shard_map/all_gather | solution.py:11
  84.5 2.5 %reduce_sum.9 = f32[256,256]{1,0:T(8,128)S(1)} reduce(f32[16,256,256]{2,1,0:T(8,128)} %bitcast.89, f32[]{:T(128)} %constant.58.clone.1), dimensions={0}, to_apply=%region_0.0 | reduce | flops 983040 | bytes 4456452 | tf_op jit(solution)/shard_map/reduce_sum | solution.py:11
  87.0 11.7 %cholesky.50 = f32[128,128]{1,0:T(8,128)S(1)} custom-call(f32[128,128]{1,0:T(8,128)S(1)} %cholesky.118), custom_call_target="Cholesky" | custom-call | tf_op jit(solution)/shard_map/cholesky | solution.py:109
  98.8 0.6 compare_reduce_fusion.1
  99.4 9.8 %custom-call.11 = f32[1,128,128]{1,2,0:T(8,128)S(1)} custom-call(f32[1,128,128]{2,1,0:T(8,128)S(1)} %get-tuple-element.41), custom_call_target="InvertDiagBlocksLowerTriangular" | custom-call | tf_op jit(solution)/shard_map/cholesky | solution.py:109
  109.2 0.2 constant_dynamic-update-slice_fusion.4
  109.4 0.3 convolution_subtract_fusion.1
  109.7 11.8 %cholesky.105 = f32[128,128]{1,0:T(8,128)S(1)} custom-call(f32[128,128]{1,0:T(8,128)S(1)} %convolution_subtract_fusion.1), custom_call_target="Cholesky" | custom-call | tf_op jit(solution)/shard_map/cholesky | solution.py:109
  121.5 0.7 compare_reduce_fusion
  123.5 0.8 copy.29
  124.4 0.1 triangular_solve.63
  124.4 3.8 %while.1 = (s32[]{:T(128)}, f32[256,256]{1,0:T(8,128)S(1)}, s32[2,2]{1,0:T(2,128)S(1)}, f32[2,128,128]{2,1,0:T(8,128)S(1)}, s32[]{:T(128)}) while((s32[]{:T(128)}, f32[256,256]{1,0:T(8,128)S(1)}, s32[2,2]{1,0:T(2,128)S(1)}, f32[2,128,128]{2,1,0:T(8,128)S(1)}, s32[]{:T(128)}) %tuple.43), condition=%wide.while_cond, body=%wide.while_body.sunk | while | flops 2 | bytes 131189 | solution.py:112
  124.4 0.6 fusion.77
  125.1 1.3 bitcast_dynamic-update-slice_fusion.2
  126.4 0.6 fusion.77
  127.0 1.3 bitcast_dynamic-update-slice_fusion.2
  128.3 19.7 %custom-call.12 = f32[2,128,128]{1,2,0:T(8,128)S(1)} custom-call(f32[2,128,128]{2,1,0:T(8,128)S(1)} %get-tuple-element.9), custom_call_target="InvertDiagBlocksLowerTriangular" | custom-call | tf_op jit(solution)/shard_map/triangular_solve | solution.py:112
  148.0 0.3 fusion.68
  148.2 0.3 convolution_subtract_fusion
  148.5 0.3 convolution_convert_fusion.1
  148.8 7.0 %convolution_convert_fusion = bf16[11520,256]{1,0:T(8,128)(2,1)} fusion(bf16[11520,256]{1,0:T(8,128)(2,1)} %bitcast.87, bf16[128,256]{1,0:T(8,128)(2,1)S(1)} %convolution_convert_fusion.1, bf16[128,256]{1,0:T(8,128)(2,1)S(1)} %get-tuple-element.52), kind=kOutput, calls=%fused_computation.2 | convolution fusion | flops 1513160704 | bytes 11927552 | tf_op jit(solution)/shard_map/dot_general | solution.py:114
  (18 shorter events, 0.3 us)
Async XLA Ops:
  7.2 77.3 %all-gather.3.cloned.1.call-start = ((), (), s32[]{:S(2)}) async-start(), calls=%async_computation | async-start | bytes 4456448 | tf_op jit(solution)/shard_map/all_gather | solution.py:11
  7.2 10.9 %collective-permute-start.1 = (f32[4,3,3,16,128]{4,3,2,1,0:T(8,128)}, f32[4,3,3,16,128]{4,3,2,1,0:T(8,128)S(1)}, u32[]{:S(2)}, u32[]{:S(2)}) collective-permute-start(f32[4,3,3,16,128]{4,3,2,1,0:T(8,128)} %param.4), channel_id=1, source_target_pairs={{1,0},{2,1},{3,2},{4,3},{5,4},{6,5},{7,6},{8,7},{9,8},{10,9},{11,1... | collective-permute-start | bytes 884744 | tf_op jit(solution)/shard_map/ppermute | solution.py:24
  7.3 9.8 %collective-permute-start = (f32[4,3,3,16,128]{4,3,2,1,0:T(8,128)}, f32[4,3,3,16,128]{4,3,2,1,0:T(8,128)S(1)}, u32[]{:S(2)}, u32[]{:S(2)}) collective-permute-start(f32[4,3,3,16,128]{4,3,2,1,0:T(8,128)} %param.4), channel_id=1, source_target_pairs={{0,1},{1,2},{2,3},{3,4},{4,5},{5,6},{6,7},{7,8},{8,9},{9,10},{10,1... | collective-permute-start | bytes 884744 | tf_op jit(solution)/shard_map/ppermute | solution.py:22
  14.8 3.9 %copy-start.1 = (bf16[3,3,10,128,256]{4,3,2,1,0:T(8,128)(2,1)S(1)}, bf16[3,3,10,128,256]{4,3,2,1,0:T(8,128)(2,1)}, u32[]{:S(2)}) copy-start(bf16[3,3,10,128,256]{4,3,2,1,0:T(8,128)(2,1)} %param.6) | copy-start | bytes 17694724
  26.3 2.5 %copy-start = (bf16[3,3,10,128,256]{4,3,2,1,0:T(8,128)(2,1)}, bf16[3,3,10,128,256]{4,3,2,1,0:T(8,128)(2,1)S(1)}, u32[]{:S(2)}) copy-start(bf16[3,3,10,128,256]{4,3,2,1,0:T(8,128)(2,1)S(1)} %add_convert_fusion) | copy-start | bytes 17694724
Sparse Core Ops, SparseCore 0:
  31.4 53.0 all-gather.2
